TPU v7x, 128 devices: a whole 4x4x4 slice. The times are simulated.
128 devices in a mesh: dof: 32 (over x, z, core), snap: 4 (over y).
Axes of the slice: x: 4, y: 4, z: 4, core: 2. Of those that a mesh axis runs over, the one named last changes fastest.
Arguments:
- snapshots: bfloat16 [131072, 1024], P('dof', 'snap')
- lengths: int32 [16], replicated, may hold values from 16 to 64, as said below
- start_block: float32 [1024, 128], replicated, may hold values from -6 to 6
Outputs:
- pod_modes: float32 [131072, 128], P(('dof', 'snap'))
- r_factor: float32 [1024, 1024], replicated
Inputs may be any that keep to these rules, and one draw needn't show every extreme that they name: `lengths`: some passage has all 64 steps active and some passage only a quarter of them.
All inputs are finite; a program needn't handle non-finite values.
Results may differ from a plain program's by a relative error of at most 0.0003.
Values may be sent and summed in bfloat16 or wider, within the bound.
No kernel may reach another device: no remote copies, remote signals or barrier semaphores. Data moves between devices by JAX's collectives and lax.ppermute only.
A program may use at most 128 MiB of HBM per device.

v0:
```python
import jax
import jax.numpy as jnp
from jax import lax
from jax.sharding import PartitionSpec as P

STEPS = 64
ITERS = 3
PASSES = 16
TILE = 128


def pack_upper(rows):
    width = rows.shape[1]
    pieces = []
    for i in range(width // TILE):
        lhs = rows[:, i * TILE : (i + 1) * TILE]
        rhs = rows[:, i * TILE :]
        pieces.append(
            lax.dot_general(lhs, rhs, (((0,), (0,)), ((), ())), preferred_element_type=jnp.float32)
        )
    return jnp.concatenate(pieces, axis=1)


def unpack_upper(packed, width):
    blocks = width // TILE
    upper_rows = []
    offset = 0
    for i in range(blocks):
        w = width - i * TILE
        piece = packed[:, offset : offset + w]
        offset += w
        upper_rows.append(jnp.pad(piece, ((0, 0), (i * TILE, 0))))
    upper = jnp.concatenate(upper_rows, axis=0)
    r = lax.broadcasted_iota(jnp.int32, (width, width), 0) // TILE
    c = lax.broadcasted_iota(jnp.int32, (width, width), 1) // TILE
    return jnp.where(r <= c, upper, upper.T)


def body(snapshots, lengths, start_block):
    rows = lax.all_to_all(snapshots, "snap", 0, 1, tiled=True)
    width = rows.shape[1]
    col_length = jnp.repeat(lengths, STEPS, total_repeat_length=width)
    columns = jnp.arange(width, dtype=jnp.int32)
    active = columns % STEPS < col_length
    masked = jnp.where(active[None, :], rows, jnp.zeros_like(rows))
    row_count = snapshots.shape[0] * lax.axis_size("dof")
    packed = lax.psum(pack_upper(masked), ("dof", "snap"))
    gram_sum = unpack_upper(packed, width)
    shifted = gram_sum / jnp.float32(row_count) + 0.05 * jnp.eye(width, dtype=jnp.float32)
    upper_factor = lax.linalg.cholesky(shifted, symmetrize_input=False).T
    contract = (((0,), (0,)), ((), ()))
    subspace = start_block
    for sweep in range(ITERS):
        image = jnp.dot(
            shifted, subspace, precision=lax.Precision.HIGHEST, preferred_element_type=jnp.float32
        )
        correlation = lax.dot_general(
            image,
            image,
            contract,
            precision=lax.Precision.HIGHEST,
            preferred_element_type=jnp.float32,
        )
        lower_factor = jnp.linalg.cholesky(correlation)
        subspace = lax.linalg.triangular_solve(
            lower_factor, image, left_side=False, lower=True, transpose_a=True
        )
    pod_modes = jnp.dot(
        masked.astype(jnp.float32),
        subspace,
        precision=lax.Precision.HIGHEST,
        preferred_element_type=jnp.float32,
    )
    return (pod_modes, upper_factor)


def solution(mesh):
    placed = (P("dof", "snap"), P(), P())
    return jax.shard_map(
        body, mesh=mesh, in_specs=placed, out_specs=(P(("dof", "snap"), None), P()), check_vma=False
    )
```

profile of v0, /device:TPU:1, one launch (start us, length us, event | category | flops | bytes accessed | tf_op | source)
XLA Modules:
  0.0 540.3 jit_solution(2373709611297239090)
XLA Ops:
  17.7 5.7 %fusion.98 = pred[1024]{0:T(1024)(128)(4,1)S(1)} fusion(pred[1024]{0:T(1024)(128)(4,1)S(1)} %get-tuple-element.30, pred[1024]{0:T(1024)(128)(4,1)S(1)} %get-tuple-element.29, pred[1024]{0:T(1024)(128)(4,1)S(1)} %get-tuple-element.28, pred[1024]{0:T(1024)(128)(4,1)S(1)} %get-tuple-element.27, pred[1024]{0:T(1024)(128)(4,1)S(1)} %get-tuple-element.26, ...), kind=kLoop, calls=%fused_computation.159 | loop fusion | flops 25600 | bytes 18500 | tf_op jit(solution)/shard_map/lt | solution.py:44
  23.4 14.4 %all-to-all-done = bf16[4,1024,256]{2,1,0:T(8,128)(2,1)S(1)} async-done(((bf16[4,1024,256]{2,1,0:T(8,128)(2,1)}), bf16[4,1024,256]{2,1,0:T(8,128)(2,1)S(1)}, u32[]{:S(2)}, u32[]{:S(2)}) %all-to-all-start) | async-done | bytes 2097184 | tf_op jit(solution)/shard_map/all_to_all | solution.py:40
  51.5 152.8 %all-reduce.10.cloned.1.call-done = f32[128,4608]{0,1:T(8,128)} async-done(((f32[128,4608]{0,1:T(8,128)}), f32[128,4608]{0,1:T(8,128)}) %all-reduce.10.cloned.1.call-update) | async-done | bytes 2359312 | tf_op jit(solution)/shard_map/psum | solution.py:47
  225.7 11.7 %cholesky.247 = f32[128,128]{1,0:T(8,128)S(1)} custom-call(f32[128,128]{1,0:T(8,128)S(1)} %cholesky.667), custom_call_target="Cholesky" | custom-call | tf_op jit(solution)/shard_map/cholesky | solution.py:50
  238.1 9.8 %custom-call.49 = f32[1,128,128]{1,2,0:T(8,128)S(1)} custom-call(f32[1,128,128]{2,1,0:T(8,128)S(1)} %get-tuple-element.54), custom_call_target="InvertDiagBlocksLowerTriangular" | custom-call | tf_op jit(solution)/shard_map/cholesky | solution.py:50
  254.5 11.7 %cholesky.636 = f32[128,128]{1,0:T(8,128)S(1)} custom-call(f32[128,128]{1,0:T(8,128)S(1)} %fusion.63), custom_call_target="Cholesky" | custom-call | tf_op jit(solution)/shard_map/jit(cholesky)/cholesky | solution.py:64
  267.5 9.8 %custom-call.58 = f32[1,128,128]{1,2,0:T(8,128)S(1)} custom-call(f32[1,128,128]{2,1,0:T(8,128)S(1)} %fusion.46), custom_call_target="InvertDiagBlocksLowerTriangular" | custom-call | tf_op jit(solution)/shard_map/triangular_solve/custom-call.16 | solution.py:65
  284.6 11.7 %cholesky.647 = f32[128,128]{1,0:T(8,128)S(1)} custom-call(f32[128,128]{1,0:T(8,128)S(1)} %fusion.61), custom_call_target="Cholesky" | custom-call | tf_op jit(solution)/shard_map/jit(cholesky)/cholesky | solution.py:64
  297.6 9.8 %custom-call.59 = f32[1,128,128]{1,2,0:T(8,128)S(1)} custom-call(f32[1,128,128]{2,1,0:T(8,128)S(1)} %fusion.47), custom_call_target="InvertDiagBlocksLowerTriangular" | custom-call | tf_op jit(solution)/shard_map/triangular_solve/custom-call.16 | solution.py:65
  314.8 11.7 %cholesky.658 = f32[128,128]{1,0:T(8,128)S(1)} custom-call(f32[128,128]{1,0:T(8,128)S(1)} %fusion.59), custom_call_target="Cholesky" | custom-call | tf_op jit(solution)/shard_map/jit(cholesky)/cholesky | solution.py:64
  327.9 9.8 %custom-call.60 = f32[1,128,128]{1,2,0:T(8,128)S(1)} custom-call(f32[1,128,128]{2,1,0:T(8,128)S(1)} %fusion.48), custom_call_target="InvertDiagBlocksLowerTriangular" | custom-call | tf_op jit(solution)/shard_map/triangular_solve/custom-call.16 | solution.py:65
  347.9 11.9 %cholesky.270 = f32[128,128]{1,0:T(8,128)S(1)} custom-call(f32[128,128]{1,0:T(8,128)S(1)} %cholesky.671), custom_call_target="Cholesky" | custom-call | tf_op jit(solution)/shard_map/cholesky | solution.py:50
  361.1 9.8 %custom-call.50 = f32[1,128,128]{1,2,0:T(8,128)S(1)} custom-call(f32[1,128,128]{2,1,0:T(8,128)S(1)} %get-tuple-element.51), custom_call_target="InvertDiagBlocksLowerTriangular" | custom-call | tf_op jit(solution)/shard_map/cholesky | solution.py:50
  374.3 11.7 %cholesky.493 = f32[128,128]{1,0:T(8,128)S(1)} custom-call(f32[128,128]{1,0:T(8,128)S(1)} %cholesky.676), custom_call_target="Cholesky" | custom-call | tf_op jit(solution)/shard_map/cholesky | solution.py:50
  387.3 10.0 %custom-call.51 = f32[1,128,128]{1,2,0:T(8,128)S(1)} custom-call(f32[1,128,128]{2,1,0:T(8,128)S(1)} %get-tuple-element.48), custom_call_target="InvertDiagBlocksLowerTriangular" | custom-call | tf_op jit(solution)/shard_map/cholesky | solution.py:50
  400.9 11.7 %cholesky.512 = f32[128,128]{1,0:T(8,128)S(1)} custom-call(f32[128,128]{1,0:T(8,128)S(1)} %cholesky.681), custom_call_target="Cholesky" | custom-call | tf_op jit(solution)/shard_map/cholesky | solution.py:50
  413.9 9.8 %custom-call.52 = f32[1,128,128]{1,2,0:T(8,128)S(1)} custom-call(f32[1,128,128]{2,1,0:T(8,128)S(1)} %get-tuple-element.45), custom_call_target="InvertDiagBlocksLowerTriangular" | custom-call | tf_op jit(solution)/shard_map/cholesky | solution.py:50
  427.1 12.1 %cholesky.531 = f32[128,128]{1,0:T(8,128)S(1)} custom-call(f32[128,128]{1,0:T(8,128)S(1)} %cholesky.686), custom_call_target="Cholesky" | custom-call | tf_op jit(solution)/shard_map/cholesky | solution.py:50
  440.5 9.8 %custom-call.53 = f32[1,128,128]{1,2,0:T(8,128)S(1)} custom-call(f32[1,128,128]{2,1,0:T(8,128)S(1)} %get-tuple-element.42), custom_call_target="InvertDiagBlocksLowerTriangular" | custom-call | tf_op jit(solution)/shard_map/cholesky | solution.py:50
  453.6 11.7 %cholesky.551 = f32[128,128]{1,0:T(8,128)S(1)} custom-call(f32[128,128]{1,0:T(8,128)S(1)} %cholesky.691), custom_call_target="Cholesky" | custom-call | tf_op jit(solution)/shard_map/cholesky | solution.py:50
  466.7 9.8 %custom-call.54 = f32[1,128,128]{1,2,0:T(8,128)S(1)} custom-call(f32[1,128,128]{2,1,0:T(8,128)S(1)} %get-tuple-element.39), custom_call_target="InvertDiagBlocksLowerTriangular" | custom-call | tf_op jit(solution)/shard_map/cholesky | solution.py:50
  479.5 11.9 %cholesky.571 = f32[128,128]{1,0:T(8,128)S(1)} custom-call(f32[128,128]{1,0:T(8,128)S(1)} %cholesky.696), custom_call_target="Cholesky" | custom-call | tf_op jit(solution)/shard_map/cholesky | solution.py:50
  492.6 9.8 %custom-call.55 = f32[1,128,128]{1,2,0:T(8,128)S(1)} custom-call(f32[1,128,128]{2,1,0:T(8,128)S(1)} %get-tuple-element.36), custom_call_target="InvertDiagBlocksLowerTriangular" | custom-call | tf_op jit(solution)/shard_map/cholesky | solution.py:50
  505.1 11.7 %cholesky.589 = f32[128,128]{1,0:T(8,128)S(1)} custom-call(f32[128,128]{1,0:T(8,128)S(1)} %convolution_subtract_fusion.6), custom_call_target="Cholesky" | custom-call | tf_op jit(solution)/shard_map/cholesky | solution.py:50
  (115 shorter events, 120.0 us)
Async XLA Ops:
  7.2 240.8 %copy-start = (f32[1024,128]{1,0:T(8,128)S(1)}, f32[1024,128]{1,0:T(8,128)}, u32[]{:S(2)}) copy-start(f32[1024,128]{1,0:T(8,128)} %param.10) | copy-start | bytes 1572868
  7.2 5.9 %copy-start.3 = (s32[8,128]{1,0:T(8,128)S(1)}, s32[8,128]{1,0:T(8,128)}, u32[]{:S(2)}) copy-start(s32[8,128]{1,0:T(8,128)} %constant.336.clone.1) | copy-start | bytes 12292
  7.2 5.2 copy-start.2
  7.2 30.6 %all-to-all-start = ((bf16[4,1024,256]{2,1,0:T(8,128)(2,1)}), bf16[4,1024,256]{2,1,0:T(8,128)(2,1)S(1)}, u32[]{:S(2)}, u32[]{:S(2)}) async-start(bf16[4,1024,256]{2,1,0:T(8,128)(2,1)} %bitcast.129), calls=%async_computation | async-start | bytes 4194304 | tf_op jit(solution)/shard_map/all_to_all | solution.py:40
  12.4 191.9 %all-reduce.10.cloned.1.call-start = ((), (), s32[]{:S(2)}) async-start(), calls=%async_computation.1 | async-start | bytes 4718592 | tf_op jit(solution)/shard_map/psum | solution.py:47
  204.3 5.7 %slice-start = ((f32[128,4608]{0,1:T(8,128)}), f32[128,640]{0,1:T(8,128)S(1)}, s32[]{:S(2)}) async-start(f32[128,4608]{0,1:T(8,128)} %all-reduce.10.cloned.1.call-done), calls=%async_computation.2 | async-start | bytes 655360 | tf_op jit(solution)/shard_map/slice | solution.py:30
  204.3 6.6 %slice-start.1 = ((f32[128,4608]{0,1:T(8,128)}), f32[128,512]{0,1:T(8,128)S(1)}, s32[]{:S(2)}) async-start(f32[128,4608]{0,1:T(8,128)} %all-reduce.10.cloned.1.call-done), calls=%async_computation.3 | async-start | bytes 524288 | tf_op jit(solution)/shard_map/slice | solution.py:30
  204.3 7.4 %slice-start.2 = ((f32[128,4608]{0,1:T(8,128)}), f32[128,384]{0,1:T(8,128)S(1)}, s32[]{:S(2)}) async-start(f32[128,4608]{0,1:T(8,128)} %all-reduce.10.cloned.1.call-done), calls=%async_computation.4 | async-start | bytes 393216 | tf_op jit(solution)/shard_map/slice | solution.py:30
  205.4 7.1 %slice-start.3 = ((f32[128,4608]{0,1:T(8,128)}), f32[128,256]{0,1:T(8,128)S(1)}, s32[]{:S(2)}) async-start(f32[128,4608]{0,1:T(8,128)} %all-reduce.10.cloned.1.call-done), calls=%async_computation.5 | async-start | bytes 262144 | tf_op jit(solution)/shard_map/slice | solution.py:30
  205.4 7.9 %slice-start.4 = ((f32[128,4608]{0,1:T(8,128)}), f32[128,128]{0,1:T(8,128)S(1)}, s32[]{:S(2)}) async-start(f32[128,4608]{0,1:T(8,128)} %all-reduce.10.cloned.1.call-done), calls=%async_computation.6 | async-start | bytes 131072 | tf_op jit(solution)/shard_map/slice | solution.py:30
  223.7 2.0 copy-start.1
Sparse Core Ops, SparseCore 0:
  51.6 152.6 all-reduce.9
where the time goes:
time: 549 us; the launch traced here: 540 us
  other arithmetic  263 us (48%)
  waiting for transfers between devices  167 us (30%)
  matrix products  57.1 us (10%)
  local copies, waits for them, and re-layouts  28.4 us (5%)
  between operations  19.6 us (4%)
    another operation x31, other arithmetic, body(): upper_factor = lax.linalg.cholesky(shifted, symmetrize_input=False).T  173 us
    psum x1, waiting for transfers between devices, body(): packed = lax.psum(pack_upper(masked), ('dof', 'snap'))  153 us
    another operation x9, other arithmetic, body(): lower_factor = jnp.linalg.cholesky(correlation)  37.2 us
    another operation x6, other arithmetic, body(): lax.linalg.triangular_solve(lower_factor, image, left_side=False, lower=T...  31.4 us
    another operation x14, matrix products, body(): upper_factor = lax.linalg.cholesky(shifted, symmetrize_input=False).T  23.1 us
    dot_general x3, matrix products, body(): jnp.dot(shifted, subspace, precision=lax.Precision.HIGHEST, preferred_ele...  16.4 us
    all_to_all x1, waiting for transfers between devices, body(): rows = lax.all_to_all(snapshots, 'snap', 0, 1, tiled=True)  14.4 us
    unnamed x16, local copies, waits for them, and re-layouts  14.2 us
  transfers between devices with their start and end apart: 2, of which 2 were waited for; matrix products, arithmetic and copies ran while one was open for 2% of the time, Pallas kernels for 0%

commit v1 on v0

--- a/solution.py
+++ b/solution.py
@@ -44,7 +44,7 @@
     active = columns % STEPS < col_length
     masked = jnp.where(active[None, :], rows, jnp.zeros_like(rows))
     row_count = snapshots.shape[0] * lax.axis_size("dof")
-    packed = lax.psum(pack_upper(masked), ("dof", "snap"))
+    packed = lax.psum(lax.psum(pack_upper(masked), "snap"), "dof")
     gram_sum = unpack_upper(packed, width)
     shifted = gram_sum / jnp.float32(row_count) + 0.05 * jnp.eye(width, dtype=jnp.float32)
     upper_factor = lax.linalg.cholesky(shifted, symmetrize_input=False).T

time: 549 us -> 567 us (1.033)
  waiting for transfers between devices: 167 us -> 190 us
    psum x1 -> x2, waiting for transfers between devices: 153 us -> 175 us  [body(): packed = lax.psum(lax.psum(pack_upper(masked), 'snap'), 'dof')]
  transfers between devices with their start and end apart: 2 -> 3, of which waited for: 2 -> 3; matrix products, arithmetic and copies ran while one was open for 2% -> 2% of each run, Pallas kernels for 0% -> 0%
where the time goes in v1:
time: 567 us; the launch traced here: 563 us
  other arithmetic  263 us (46%)
  waiting for transfers between devices  190 us (34%)
  matrix products  57.1 us (10%)
  local copies, waits for them, and re-layouts  28.4 us (5%)
  between operations  19.7 us (3%)
    psum x2, waiting for transfers between devices, body(): packed = lax.psum(lax.psum(pack_upper(masked), 'snap'), 'dof')  175 us
    another operation x31, other arithmetic, body(): upper_factor = lax.linalg.cholesky(shifted, symmetrize_input=False).T  173 us
    another operation x9, other arithmetic, body(): lower_factor = jnp.linalg.cholesky(correlation)  37.2 us
    another operation x6, other arithmetic, body(): lax.linalg.triangular_solve(lower_factor, image, left_side=False, lower=T...  31.4 us
    another operation x14, matrix products, body(): upper_factor = lax.linalg.cholesky(shifted, symmetrize_input=False).T  23.2 us
    dot_general x3, matrix products, body(): jnp.dot(shifted, subspace, precision=lax.Precision.HIGHEST, preferred_ele...  16.4 us
    all_to_all x1, waiting for transfers between devices, body(): rows = lax.all_to_all(snapshots, 'snap', 0, 1, tiled=True)  14.4 us
    unnamed x16, local copies, waits for them, and re-layouts  14.2 us
  transfers between devices with their start and end apart: 3, of which 3 were waited for; matrix products, arithmetic and copies ran while one was open for 2% of the time, Pallas kernels for 0%

profile of v1, /device:TPU:1, one launch (start us, length us, event | category | flops | bytes accessed | tf_op | source)
XLA Modules:
  0.0 563.0 jit_solution(17462333356909838093)
XLA Ops:
  23.4 14.4 %all-to-all-done = bf16[4,1024,256]{2,1,0:T(8,128)(2,1)S(1)} async-done(((bf16[4,1024,256]{2,1,0:T(8,128)(2,1)}), bf16[4,1024,256]{2,1,0:T(8,128)(2,1)S(1)}, u32[]{:S(2)}, u32[]{:S(2)}) %all-to-all-start) | async-done | bytes 2097184 | tf_op jit(solution)/shard_map/all_to_all | solution.py:40
  51.7 64.5 %all-reduce.11.cloned.1.call-done = f32[128,4608]{0,1:T(8,128)} async-done(((f32[128,4608]{0,1:T(8,128)}), f32[128,4608]{0,1:T(8,128)}) %all-reduce.11.cloned.1.call-update) | async-done | bytes 2359312 | tf_op jit(solution)/shard_map/psum | solution.py:47
  116.2 110.7 %all-reduce.13.cloned.1.call-done = f32[128,4608]{0,1:T(8,128)} async-done(((f32[128,4608]{0,1:T(8,128)}), f32[128,4608]{0,1:T(8,128)}) %all-reduce.13.cloned.1.call-update) | async-done | bytes 2359312 | tf_op jit(solution)/shard_map/psum | solution.py:47
  248.4 11.7 %cholesky.247 = f32[128,128]{1,0:T(8,128)S(1)} custom-call(f32[128,128]{1,0:T(8,128)S(1)} %cholesky.667), custom_call_target="Cholesky" | custom-call | tf_op jit(solution)/shard_map/cholesky | solution.py:50
  260.8 9.8 %custom-call.49 = f32[1,128,128]{1,2,0:T(8,128)S(1)} custom-call(f32[1,128,128]{2,1,0:T(8,128)S(1)} %get-tuple-element.54), custom_call_target="InvertDiagBlocksLowerTriangular" | custom-call | tf_op jit(solution)/shard_map/cholesky | solution.py:50
  277.2 11.7 %cholesky.636 = f32[128,128]{1,0:T(8,128)S(1)} custom-call(f32[128,128]{1,0:T(8,128)S(1)} %fusion.63), custom_call_target="Cholesky" | custom-call | tf_op jit(solution)/shard_map/jit(cholesky)/cholesky | solution.py:64
  290.2 9.8 %custom-call.58 = f32[1,128,128]{1,2,0:T(8,128)S(1)} custom-call(f32[1,128,128]{2,1,0:T(8,128)S(1)} %fusion.46), custom_call_target="InvertDiagBlocksLowerTriangular" | custom-call | tf_op jit(solution)/shard_map/triangular_solve/custom-call.16 | solution.py:65
  307.5 11.7 %cholesky.647 = f32[128,128]{1,0:T(8,128)S(1)} custom-call(f32[128,128]{1,0:T(8,128)S(1)} %fusion.61), custom_call_target="Cholesky" | custom-call | tf_op jit(solution)/shard_map/jit(cholesky)/cholesky | solution.py:64
  320.5 9.8 %custom-call.59 = f32[1,128,128]{1,2,0:T(8,128)S(1)} custom-call(f32[1,128,128]{2,1,0:T(8,128)S(1)} %fusion.47), custom_call_target="InvertDiagBlocksLowerTriangular" | custom-call | tf_op jit(solution)/shard_map/triangular_solve/custom-call.16 | solution.py:65
  337.5 11.7 %cholesky.658 = f32[128,128]{1,0:T(8,128)S(1)} custom-call(f32[128,128]{1,0:T(8,128)S(1)} %fusion.59), custom_call_target="Cholesky" | custom-call | tf_op jit(solution)/shard_map/jit(cholesky)/cholesky | solution.py:64
  350.6 9.8 %custom-call.60 = f32[1,128,128]{1,2,0:T(8,128)S(1)} custom-call(f32[1,128,128]{2,1,0:T(8,128)S(1)} %fusion.48), custom_call_target="InvertDiagBlocksLowerTriangular" | custom-call | tf_op jit(solution)/shard_map/triangular_solve/custom-call.16 | solution.py:65
  370.6 11.9 %cholesky.270 = f32[128,128]{1,0:T(8,128)S(1)} custom-call(f32[128,128]{1,0:T(8,128)S(1)} %cholesky.671), custom_call_target="Cholesky" | custom-call | tf_op jit(solution)/shard_map/cholesky | solution.py:50
  383.8 9.8 %custom-call.50 = f32[1,128,128]{1,2,0:T(8,128)S(1)} custom-call(f32[1,128,128]{2,1,0:T(8,128)S(1)} %get-tuple-element.51), custom_call_target="InvertDiagBlocksLowerTriangular" | custom-call | tf_op jit(solution)/shard_map/cholesky | solution.py:50
  397.0 11.7 %cholesky.493 = f32[128,128]{1,0:T(8,128)S(1)} custom-call(f32[128,128]{1,0:T(8,128)S(1)} %cholesky.676), custom_call_target="Cholesky" | custom-call | tf_op jit(solution)/shard_map/cholesky | solution.py:50
  410.1 10.2 %custom-call.51 = f32[1,128,128]{1,2,0:T(8,128)S(1)} custom-call(f32[1,128,128]{2,1,0:T(8,128)S(1)} %get-tuple-element.48), custom_call_target="InvertDiagBlocksLowerTriangular" | custom-call | tf_op jit(solution)/shard_map/cholesky | solution.py:50
  423.8 11.7 %cholesky.512 = f32[128,128]{1,0:T(8,128)S(1)} custom-call(f32[128,128]{1,0:T(8,128)S(1)} %cholesky.681), custom_call_target="Cholesky" | custom-call | tf_op jit(solution)/shard_map/cholesky | solution.py:50
  436.8 9.8 %custom-call.52 = f32[1,128,128]{1,2,0:T(8,128)S(1)} custom-call(f32[1,128,128]{2,1,0:T(8,128)S(1)} %get-tuple-element.45), custom_call_target="InvertDiagBlocksLowerTriangular" | custom-call | tf_op jit(solution)/shard_map/cholesky | solution.py:50
  450.0 11.8 %cholesky.531 = f32[128,128]{1,0:T(8,128)S(1)} custom-call(f32[128,128]{1,0:T(8,128)S(1)} %cholesky.686), custom_call_target="Cholesky" | custom-call | tf_op jit(solution)/shard_map/cholesky | solution.py:50
  463.1 9.8 %custom-call.53 = f32[1,128,128]{1,2,0:T(8,128)S(1)} custom-call(f32[1,128,128]{2,1,0:T(8,128)S(1)} %get-tuple-element.42), custom_call_target="InvertDiagBlocksLowerTriangular" | custom-call | tf_op jit(solution)/shard_map/cholesky | solution.py:50
  476.3 11.7 %cholesky.551 = f32[128,128]{1,0:T(8,128)S(1)} custom-call(f32[128,128]{1,0:T(8,128)S(1)} %cholesky.691), custom_call_target="Cholesky" | custom-call | tf_op jit(solution)/shard_map/cholesky | solution.py:50
  489.3 9.8 %custom-call.54 = f32[1,128,128]{1,2,0:T(8,128)S(1)} custom-call(f32[1,128,128]{2,1,0:T(8,128)S(1)} %get-tuple-element.39), custom_call_target="InvertDiagBlocksLowerTriangular" | custom-call | tf_op jit(solution)/shard_map/cholesky | solution.py:50
  502.1 11.9 %cholesky.571 = f32[128,128]{1,0:T(8,128)S(1)} custom-call(f32[128,128]{1,0:T(8,128)S(1)} %cholesky.696), custom_call_target="Cholesky" | custom-call | tf_op jit(solution)/shard_map/cholesky | solution.py:50
  515.4 9.8 %custom-call.55 = f32[1,128,128]{1,2,0:T(8,128)S(1)} custom-call(f32[1,128,128]{2,1,0:T(8,128)S(1)} %get-tuple-element.36), custom_call_target="InvertDiagBlocksLowerTriangular" | custom-call | tf_op jit(solution)/shard_map/cholesky | solution.py:50
  527.8 11.7 %cholesky.589 = f32[128,128]{1,0:T(8,128)S(1)} custom-call(f32[128,128]{1,0:T(8,128)S(1)} %convolution_subtract_fusion.6), custom_call_target="Cholesky" | custom-call | tf_op jit(solution)/shard_map/cholesky | solution.py:50
  (118 shorter events, 126.0 us)
Async XLA Ops:
  7.2 263.4 %copy-start = (f32[1024,128]{1,0:T(8,128)S(1)}, f32[1024,128]{1,0:T(8,128)}, u32[]{:S(2)}) copy-start(f32[1024,128]{1,0:T(8,128)} %param.10) | copy-start | bytes 1572868
  7.2 5.9 %copy-start.3 = (s32[8,128]{1,0:T(8,128)S(1)}, s32[8,128]{1,0:T(8,128)}, u32[]{:S(2)}) copy-start(s32[8,128]{1,0:T(8,128)} %constant.336.clone.1) | copy-start | bytes 12292
  7.2 5.2 copy-start.2
  7.2 30.6 %all-to-all-start = ((bf16[4,1024,256]{2,1,0:T(8,128)(2,1)}), bf16[4,1024,256]{2,1,0:T(8,128)(2,1)S(1)}, u32[]{:S(2)}, u32[]{:S(2)}) async-start(bf16[4,1024,256]{2,1,0:T(8,128)(2,1)} %bitcast.129), calls=%async_computation | async-start | bytes 4194304 | tf_op jit(solution)/shard_map/all_to_all | solution.py:40
  12.4 103.8 %all-reduce.11.cloned.1.call-start = ((), (), s32[]{:S(2)}) async-start(), calls=%async_computation.1 | async-start | bytes 4718592 | tf_op jit(solution)/shard_map/psum | solution.py:47
  51.4 175.5 %all-reduce.13.cloned.1.call-start = ((), (), s32[]{:S(2)}) async-start(), calls=%async_computation.2 | async-start | bytes 4718592 | tf_op jit(solution)/shard_map/psum | solution.py:47
  226.9 5.7 %slice-start = ((f32[128,4608]{0,1:T(8,128)}), f32[128,640]{0,1:T(8,128)S(1)}, s32[]{:S(2)}) async-start(f32[128,4608]{0,1:T(8,128)} %all-reduce.13.cloned.1.call-done), calls=%async_computation.3 | async-start | bytes 655360 | tf_op jit(solution)/shard_map/slice | solution.py:30
  226.9 6.6 %slice-start.1 = ((f32[128,4608]{0,1:T(8,128)}), f32[128,512]{0,1:T(8,128)S(1)}, s32[]{:S(2)}) async-start(f32[128,4608]{0,1:T(8,128)} %all-reduce.13.cloned.1.call-done), calls=%async_computation.4 | async-start | bytes 524288 | tf_op jit(solution)/shard_map/slice | solution.py:30
  226.9 7.4 %slice-start.2 = ((f32[128,4608]{0,1:T(8,128)}), f32[128,384]{0,1:T(8,128)S(1)}, s32[]{:S(2)}) async-start(f32[128,4608]{0,1:T(8,128)} %all-reduce.13.cloned.1.call-done), calls=%async_computation.5 | async-start | bytes 393216 | tf_op jit(solution)/shard_map/slice | solution.py:30
  228.1 7.1 %slice-start.3 = ((f32[128,4608]{0,1:T(8,128)}), f32[128,256]{0,1:T(8,128)S(1)}, s32[]{:S(2)}) async-start(f32[128,4608]{0,1:T(8,128)} %all-reduce.13.cloned.1.call-done), calls=%async_computation.6 | async-start | bytes 262144 | tf_op jit(solution)/shard_map/slice | solution.py:30
  228.1 7.9 %slice-start.4 = ((f32[128,4608]{0,1:T(8,128)}), f32[128,128]{0,1:T(8,128)S(1)}, s32[]{:S(2)}) async-start(f32[128,4608]{0,1:T(8,128)} %all-reduce.13.cloned.1.call-done), calls=%async_computation.7 | async-start | bytes 131072 | tf_op jit(solution)/shard_map/slice | solution.py:30
  246.4 2.0 copy-start.1
Sparse Core Ops, SparseCore 0:
  51.6 64.5 all-reduce.10
  119.5 107.4 all-reduce.12
